TPU v7x, 256 devices: a whole 4x4x8 slice. The times are simulated.
256 devices in a mesh: ta: 4 (over y), gz: 8 (over x, core), xy: 8 (over z).
Axes of the slice: x: 4, y: 4, z: 8, core: 2. Of those that a mesh axis runs over, the one named last changes fastest.
Arguments:
- right_side: bfloat16 [8, 16, 16, 2, 16, 128], P('ta', 'gz', 'xy'), may hold values from -40 to 40
- links: bfloat16 [8, 16, 16, 2, 9, 64, 128], P('ta', 'gz', 'xy'), may hold values from -4 to 8, as said below
Outputs:
- solution: float32 [8, 16, 16, 2, 16, 128], P('ta', 'gz', 'xy')
Inputs may be any that keep to these rules, and one draw needn't show every extreme that they name: `links`: block entries; block 0 acts on the site itself.
All inputs are finite; a program needn't handle non-finite values.
Results may differ from a plain program's by a relative error of at most 0.008.
Values may be sent and summed in bfloat16 or wider, within the bound.
No kernel may reach another device: no remote copies, remote signals or barrier semaphores. Data moves between devices by JAX's collectives and lax.ppermute only.
A program may use at most 64 MiB of HBM per device.

v0:
```python
import jax
import jax.numpy as jnp
from jax import lax
from jax.sharding import PartitionSpec as P

ITERS = 3
EPSILON = 1e-06


def extended(value, sides, width):
    for axis, dim in sides:
        size, length = (lax.axis_size(axis), value.shape[dim])
        up = [(i, (i + 1) % size) for i in range(size)]
        down = [(j, i) for i, j in up]
        last = lax.slice_in_dim(value, length - width, length, axis=dim)
        first = lax.slice_in_dim(value, 0, width, axis=dim)
        before = lax.ppermute(last, axis, up)
        after = lax.ppermute(first, axis, down)
        value = jnp.concatenate([before, value, after], axis=dim)
    return value


def turned(field):
    half = field.shape[-1] // 2
    return jnp.concatenate([-field[..., half:], field[..., :half]], axis=-1)


def inner_pair(left, right):
    return (
        jnp.sum(left * right, axis=(0, 1, 2, 3, 5)),
        jnp.sum(turned(left) * right, axis=(0, 1, 2, 3, 5)),
    )


def combined(coef_re, coef_im, field):
    return coef_re[:, None] * field + coef_im[:, None] * turned(field)


def global_squares(field):
    return lax.psum(jnp.sum(field * field, axis=(0, 1, 2, 3, 5)), ("ta", "gz", "xy"))


def hop_products(padded, blocks, half):
    here = padded[1:-1, 1:-1, 1:-1]
    near = jnp.stack(
        [
            here,
            padded[2:, 1:-1, 1:-1],
            padded[:-2, 1:-1, 1:-1],
            padded[1:-1, 2:, 1:-1],
            padded[1:-1, :-2, 1:-1],
            padded[1:-1, 1:-1, 2:],
            padded[1:-1, 1:-1, :-2],
            jnp.roll(here, -1, 3),
            jnp.roll(here, 1, 3),
        ],
        axis=0,
    )
    real_half = near[..., :half]
    imag_half = near[..., half:]
    paired = jnp.stack(
        [
            jnp.concatenate([real_half, -imag_half], axis=-1),
            jnp.concatenate([imag_half, real_half], axis=-1),
        ],
        axis=-3,
    )
    paired = paired.reshape(9, blocks.shape[0], 2, here.shape[4], here.shape[5])
    output = jnp.einsum("sbkj,bscrj->srck", blocks, paired, preferred_element_type=jnp.float32)
    return output.reshape(here.shape).astype(jnp.bfloat16)


def least_squares(rows_re, rows_im, start_norm):
    count = len(rows_re[0])
    height_re = jnp.transpose(jnp.stack([jnp.stack(row) for row in rows_re]), (2, 0, 1))
    height_im = jnp.transpose(jnp.stack([jnp.stack(row) for row in rows_im]), (2, 0, 1))
    upper = jnp.concatenate([height_re, -height_im], axis=2)
    lower = jnp.concatenate([height_im, height_re], axis=2)
    stacked = jnp.concatenate([upper, lower], axis=1)
    normal = jnp.einsum("rik,rij->rkj", stacked, stacked, precision=lax.Precision.HIGHEST)
    target = start_norm[:, None] * stacked[:, 0, :]
    factor = jnp.linalg.cholesky(normal)
    middle = lax.linalg.triangular_solve(factor, target[:, :, None], left_side=True, lower=True)
    coefs = lax.linalg.triangular_solve(
        factor, middle, left_side=True, lower=True, transpose_a=True
    )[:, :, 0]
    return (coefs[:, :count], coefs[:, count:])


def on_device(right_side, links):
    dims = right_side.shape
    half = dims[5] // 2
    sites = dims[0] * dims[1] * dims[2] * dims[3]
    blocks = links.reshape(sites, 9, half, dims[5])
    source = right_side.astype(jnp.float32)
    start_norm = jnp.sqrt(global_squares(source) + EPSILON)
    basis = [source / start_norm[:, None]]
    zero_row = jnp.zeros_like(start_norm)
    rows_re = [[zero_row for column in range(ITERS)] for height in range(ITERS + 1)]
    rows_im = [[zero_row for column in range(ITERS)] for height in range(ITERS + 1)]
    for column in range(ITERS):
        padded = extended(basis[column].astype(jnp.bfloat16), (("ta", 0), ("gz", 1), ("xy", 2)), 1)
        residue = hop_products(padded, blocks, half).astype(jnp.float32)
        for earlier in range(column + 1):
            proj_re, proj_im = lax.psum(inner_pair(basis[earlier], residue), ("ta", "gz", "xy"))
            rows_re[earlier][column] = proj_re
            rows_im[earlier][column] = proj_im
            residue = residue - combined(proj_re, proj_im, basis[earlier])
        length = jnp.sqrt(global_squares(residue) + EPSILON)
        rows_re[column + 1][column] = length
        if column + 1 < ITERS:
            basis.append(residue / length[:, None])
    coef_re, coef_im = least_squares(rows_re, rows_im, start_norm)
    solution = jnp.zeros(dims, jnp.float32)
    for column in range(ITERS):
        solution = solution + combined(coef_re[:, column], coef_im[:, column], basis[column])
    return solution


def solution(mesh):
    in_specs = (P("ta", "gz", "xy", None, None, None), P("ta", "gz", "xy", None, None, None, None))
    out_specs = P("ta", "gz", "xy", None, None, None)
    return jax.shard_map(
        on_device, mesh=mesh, in_specs=in_specs, out_specs=out_specs, check_vma=False
    )
```

profile of v0, /device:TPU:1, one launch (start us, length us, event | category | flops | bytes accessed | tf_op | source)
XLA Modules:
  0.0 832.7 jit_solution(8448418020664260992)
XLA Ops:
  1.1 81.4 %psum.112 = f32[16]{0:T(128)S(1)} all-reduce(f32[16]{0:T(128)S(1)} %fusion.48), channel_id=1, replica_groups=mesh['ta'=4,'gz'=8,'xy'=8] {'ta','gz','xy'}, use_global_device_ids=true, to_apply=%region_1.0 | all-reduce | flops 16 | bytes 128 | tf_op jit(solution)/shard_map/psum | solution.py:40
  85.1 1.2 collective-permute-done
  86.3 1.7 collective-permute-done.1
  88.1 2.1 collective-permute-start.2
  91.4 1.9 collective-permute-done.2
  94.9 2.3 collective-permute-done.4
  97.2 1.8 collective-permute-done.5
  102.2 74.0 %all-reduce.7 = (f32[16]{0:T(128)S(1)}, f32[16]{0:T(128)S(1)}) all-reduce(f32[16]{0:T(128)S(1)} %multiply_reduce_fusion.2, f32[16]{0:T(128)S(1)} %get-tuple-element.74), channel_id=1, replica_groups=mesh['ta'=4,'gz'=8,'xy'=8] {'ta','gz','xy'}, use_global_device_ids=true, to_apply=%region_5.6 | all-reduce | flops 32 | bytes 256 | tf_op jit(solution)/shard_map/psum | solution.py:105
  176.4 74.4 %psum.115 = f32[16]{0:T(128)S(1)} all-reduce(f32[16]{0:T(128)S(1)} %get-tuple-element.37), channel_id=1, replica_groups=mesh['ta'=4,'gz'=8,'xy'=8] {'ta','gz','xy'}, use_global_device_ids=true, to_apply=%region_7.8 | all-reduce | flops 16 | bytes 128 | tf_op jit(solution)/shard_map/psum | solution.py:40
  250.9 2.3 collective-permute-start.6
  254.2 3.0 collective-permute-done.7
  257.2 2.1 collective-permute-start.8
  259.4 1.5 collective-permute-done.8
  262.6 2.3 collective-permute-done.10
  264.9 2.1 collective-permute-done.11
  269.7 75.2 %all-reduce.6 = (f32[16]{0:T(128)S(1)}, f32[16]{0:T(128)S(1)}) all-reduce(f32[16]{0:T(128)S(1)} %get-tuple-element.100, f32[16]{0:T(128)S(1)} %multiply_reduce_fusion.12), channel_id=1, replica_groups=mesh['ta'=4,'gz'=8,'xy'=8] {'ta','gz','xy'}, use_global_device_ids=true, to_apply=%region_11.12 | all-reduce | flops 32 | bytes 256 | tf_op jit(solution)/shard_map/psum | solution.py:105
  344.9 1.2 multiply_reduce_fusion.11
  346.0 74.4 %all-reduce.5 = (f32[16]{0:T(128)S(1)}, f32[16]{0:T(128)S(1)}) all-reduce(f32[16]{0:T(128)S(1)} %get-tuple-element.10, f32[16]{0:T(128)S(1)} %get-tuple-element.9), channel_id=1, replica_groups=mesh['ta'=4,'gz'=8,'xy'=8] {'ta','gz','xy'}, use_global_device_ids=true, to_apply=%region_15.16 | all-reduce | flops 32 | bytes 256 | tf_op jit(solution)/shard_map/psum | solution.py:105
  420.6 73.4 %psum.120 = f32[16]{0:T(128)S(1)} all-reduce(f32[16]{0:T(128)S(1)} %get-tuple-element.30), channel_id=1, replica_groups=mesh['ta'=4,'gz'=8,'xy'=8] {'ta','gz','xy'}, use_global_device_ids=true, to_apply=%region_17.18 | all-reduce | flops 16 | bytes 128 | tf_op jit(solution)/shard_map/psum | solution.py:40
  494.1 2.4 collective-permute-start.12
  497.6 3.0 collective-permute-done.13
  500.6 2.1 collective-permute-start.14
  502.7 1.5 collective-permute-done.14
  504.3 1.8 collective-permute-start.16
  506.3 2.2 collective-permute-done.16
  508.5 2.7 collective-permute-done.17
  515.5 75.2 %all-reduce.4 = (f32[16]{0:T(128)S(1)}, f32[16]{0:T(128)S(1)}) all-reduce(f32[16]{0:T(128)S(1)} %get-tuple-element.102, f32[16]{0:T(128)S(1)} %multiply_reduce_fusion.8), channel_id=1, replica_groups=mesh['ta'=4,'gz'=8,'xy'=8] {'ta','gz','xy'}, use_global_device_ids=true, to_apply=%region_21.22 | all-reduce | flops 32 | bytes 256 | tf_op jit(solution)/shard_map/psum | solution.py:105
  590.9 74.6 %all-reduce.3 = (f32[16]{0:T(128)S(1)}, f32[16]{0:T(128)S(1)}) all-reduce(f32[16]{0:T(128)S(1)} %get-tuple-element.8, f32[16]{0:T(128)S(1)} %get-tuple-element.7), channel_id=1, replica_groups=mesh['ta'=4,'gz'=8,'xy'=8] {'ta','gz','xy'}, use_global_device_ids=true, to_apply=%region_25.26 | all-reduce | flops 32 | bytes 256 | tf_op jit(solution)/shard_map/psum | solution.py:105
  665.7 73.4 %all-reduce.2 = (f32[16]{0:T(128)S(1)}, f32[16]{0:T(128)S(1)}) all-reduce(f32[16]{0:T(128)S(1)} %get-tuple-element.6, f32[16]{0:T(128)S(1)} %get-tuple-element.5), channel_id=1, replica_groups=mesh['ta'=4,'gz'=8,'xy'=8] {'ta','gz','xy'}, use_global_device_ids=true, to_apply=%region_29.30 | all-reduce | flops 32 | bytes 256 | tf_op jit(solution)/shard_map/psum | solution.py:105
  739.4 74.2 %psum.127 = f32[16]{0:T(128)S(1)} all-reduce(f32[16]{0:T(128)S(1)} %multiply_reduce_fusion.3), channel_id=1, replica_groups=mesh['ta'=4,'gz'=8,'xy'=8] {'ta','gz','xy'}, use_global_device_ids=true, to_apply=%region_31.32 | all-reduce | flops 16 | bytes 128 | tf_op jit(solution)/shard_map/psum | solution.py:40
  814.5 8.8 %custom-call.9 = f32[16,6,6]{2,1,0:T(8,128)S(1)} custom-call(f32[16,6,6]{2,1,0:T(8,128)S(1)} %fusion.88), custom_call_target="Cholesky" | custom-call | tf_op jit(solution)/shard_map/jit(cholesky)/cholesky | solution.py:82
  823.6 7.6 custom-call.10
  (142 shorter events, 24.5 us)
Async XLA Ops:
  0.0 100.2 %copy-start = (bf16[2,2,2,2,9,64,128]{6,5,4,3,2,1,0:T(8,128)(2,1)S(1)}, bf16[2,2,2,2,9,64,128]{6,5,4,3,2,1,0:T(8,128)(2,1)}, u32[]{:S(2)}) copy-start(bf16[2,2,2,2,9,64,128]{6,5,4,3,2,1,0:T(8,128)(2,1)} %param.3) | copy-start | bytes 7077892
  83.5 2.8 collective-permute-start
  84.1 4.0 collective-permute-start.1
  88.1 5.2 collective-permute-start.2
  90.2 3.1 collective-permute-start.3
  93.3 3.9 collective-permute-start.4
  94.0 5.0 collective-permute-start.5
  100.2 1.2 copy-start.1
  250.9 3.4 collective-permute-start.6
  253.2 4.0 collective-permute-start.7
  257.2 3.7 collective-permute-start.8
  259.4 1.6 collective-permute-start.9
  261.0 3.9 collective-permute-start.10
  262.0 5.0 collective-permute-start.11
  494.1 3.4 collective-permute-start.12
  496.5 4.0 collective-permute-start.13
  500.6 3.7 collective-permute-start.14
  502.7 1.6 collective-permute-start.15
  504.3 4.2 collective-permute-start.16
  506.2 5.0 collective-permute-start.17
where the time goes:
time: 834 us; the launch traced here: 833 us
  blocking collectives  750 us (90%)
  waiting for transfers between devices  28.3 us (3%)
  other arithmetic  27.2 us (3%)
  starting transfers between devices  18.8 us (2%)
    psum x6, blocking collectives, on_device(): lax.psum(inner_pair(basis[earlier], residue), ('ta', 'gz', 'xy'))  447 us
    psum x4, blocking collectives, global_squares(): lax.psum(jnp.sum(field * field, axis=(0, 1, 2, 3, 5)), ('ta', 'gz', 'xy'))  303 us
  transfers between devices with their start and end apart: 18, of which 15 were waited for; matrix products, arithmetic and copies ran while one was open for 0% of the time, Pallas kernels for 0%

commit v1 on v0

--- a/solution.py
+++ b/solution.py
@@ -37,7 +37,9 @@
 
 
 def global_squares(field):
-    return lax.psum(jnp.sum(field * field, axis=(0, 1, 2, 3, 5)), ("ta", "gz", "xy"))
+    return jnp.sum(
+        lax.all_gather(jnp.sum(field * field, axis=(0, 1, 2, 3, 5)), ("ta", "gz", "xy")), axis=0
+    )
 
 
 def hop_products(padded, blocks, half):

time: 834 us -> 836 us (level)
    unnamed x0 -> x4, blocking collectives: none -> 303 us
    psum x4 -> x0, blocking collectives: 303 us -> none  [global_squares(): lax.psum(jnp.sum(field * field, axis=(0, 1, 2, 3, 5)), ('ta', 'gz', 'xy'))]
where the time goes in v1:
time: 836 us; the launch traced here: 835 us
  blocking collectives  750 us (90%)
  waiting for transfers between devices  28.3 us (3%)
  other arithmetic  27.5 us (3%)
  starting transfers between devices  18.9 us (2%)
    psum x6, blocking collectives, on_device(): lax.psum(inner_pair(basis[earlier], residue), ('ta', 'gz', 'xy'))  447 us
    unnamed x4, blocking collectives  303 us
  transfers between devices with their start and end apart: 18, of which 15 were waited for; matrix products, arithmetic and copies ran while one was open for 0% of the time, Pallas kernels for 0%

profile of v1, /device:TPU:1, one launch (start us, length us, event | category | flops | bytes accessed | tf_op | source)
XLA Modules:
  0.0 834.6 jit_solution(9074701247139356117)
XLA Ops:
  1.4 81.4 %all-reduce.2 = f32[4096]{0:T(1024)S(1)} all-reduce(f32[4096]{0:T(1024)S(1)} %dynamic-update-slice.3), channel_id=2, replica_groups=mesh['ta'=4,'gz'=8,'xy'=8] {'ta','gz','xy'}, use_global_device_ids=true, to_apply=%add.2 | all-reduce | flops 4096 | bytes 32768
  85.6 1.2 collective-permute-done
  86.8 1.7 collective-permute-done.1
  88.5 2.1 collective-permute-start.2
  91.8 1.9 collective-permute-done.2
  95.4 2.3 collective-permute-done.4
  97.7 1.7 collective-permute-done.5
  102.6 74.0 %all-reduce.11 = (f32[16]{0:T(128)S(1)}, f32[16]{0:T(128)S(1)}) all-reduce(f32[16]{0:T(128)S(1)} %multiply_reduce_fusion.2, f32[16]{0:T(128)S(1)} %get-tuple-element.74), channel_id=1, replica_groups=mesh['ta'=4,'gz'=8,'xy'=8] {'ta','gz','xy'}, use_global_device_ids=true, to_apply=%region_5.6 | all-reduce | flops 32 | bytes 256 | tf_op jit(solution)/shard_map/psum | solution.py:107
  177.1 74.4 %all-reduce.3 = f32[4096]{0:T(1024)S(1)} all-reduce(f32[4096]{0:T(1024)S(1)} %dynamic-update-slice.4), channel_id=3, replica_groups=mesh['ta'=4,'gz'=8,'xy'=8] {'ta','gz','xy'}, use_global_device_ids=true, to_apply=%add.3 | all-reduce | flops 4096 | bytes 32768
  251.8 2.4 collective-permute-start.6
  255.2 3.0 collective-permute-done.7
  258.2 2.1 collective-permute-start.8
  260.3 1.5 collective-permute-done.8
  263.5 2.3 collective-permute-done.10
  265.8 2.1 collective-permute-done.11
  270.6 75.2 %all-reduce.10 = (f32[16]{0:T(128)S(1)}, f32[16]{0:T(128)S(1)}) all-reduce(f32[16]{0:T(128)S(1)} %get-tuple-element.100, f32[16]{0:T(128)S(1)} %multiply_reduce_fusion.12), channel_id=1, replica_groups=mesh['ta'=4,'gz'=8,'xy'=8] {'ta','gz','xy'}, use_global_device_ids=true, to_apply=%region_11.12 | all-reduce | flops 32 | bytes 256 | tf_op jit(solution)/shard_map/psum | solution.py:107
  345.8 1.2 multiply_reduce_fusion.11
  347.0 74.4 %all-reduce.9 = (f32[16]{0:T(128)S(1)}, f32[16]{0:T(128)S(1)}) all-reduce(f32[16]{0:T(128)S(1)} %get-tuple-element.10, f32[16]{0:T(128)S(1)} %get-tuple-element.9), channel_id=1, replica_groups=mesh['ta'=4,'gz'=8,'xy'=8] {'ta','gz','xy'}, use_global_device_ids=true, to_apply=%region_15.16 | all-reduce | flops 32 | bytes 256 | tf_op jit(solution)/shard_map/psum | solution.py:107
  421.8 73.4 %all-reduce.4 = f32[4096]{0:T(1024)S(1)} all-reduce(f32[4096]{0:T(1024)S(1)} %dynamic-update-slice.5), channel_id=4, replica_groups=mesh['ta'=4,'gz'=8,'xy'=8] {'ta','gz','xy'}, use_global_device_ids=true, to_apply=%add.4 | all-reduce | flops 4096 | bytes 32768
  495.5 2.4 collective-permute-start.12
  499.0 3.0 collective-permute-done.13
  502.0 2.1 collective-permute-start.14
  504.1 1.5 collective-permute-done.14
  505.8 1.8 collective-permute-start.16
  507.7 2.2 collective-permute-done.16
  510.0 2.7 collective-permute-done.17
  516.9 75.2 %all-reduce.8 = (f32[16]{0:T(128)S(1)}, f32[16]{0:T(128)S(1)}) all-reduce(f32[16]{0:T(128)S(1)} %get-tuple-element.102, f32[16]{0:T(128)S(1)} %multiply_reduce_fusion.8), channel_id=1, replica_groups=mesh['ta'=4,'gz'=8,'xy'=8] {'ta','gz','xy'}, use_global_device_ids=true, to_apply=%region_21.22 | all-reduce | flops 32 | bytes 256 | tf_op jit(solution)/shard_map/psum | solution.py:107
  592.4 74.6 %all-reduce.7 = (f32[16]{0:T(128)S(1)}, f32[16]{0:T(128)S(1)}) all-reduce(f32[16]{0:T(128)S(1)} %get-tuple-element.8, f32[16]{0:T(128)S(1)} %get-tuple-element.7), channel_id=1, replica_groups=mesh['ta'=4,'gz'=8,'xy'=8] {'ta','gz','xy'}, use_global_device_ids=true, to_apply=%region_25.26 | all-reduce | flops 32 | bytes 256 | tf_op jit(solution)/shard_map/psum | solution.py:107
  667.2 73.4 %all-reduce.6 = (f32[16]{0:T(128)S(1)}, f32[16]{0:T(128)S(1)}) all-reduce(f32[16]{0:T(128)S(1)} %get-tuple-element.6, f32[16]{0:T(128)S(1)} %get-tuple-element.5), channel_id=1, replica_groups=mesh['ta'=4,'gz'=8,'xy'=8] {'ta','gz','xy'}, use_global_device_ids=true, to_apply=%region_29.30 | all-reduce | flops 32 | bytes 256 | tf_op jit(solution)/shard_map/psum | solution.py:107
  741.1 74.3 %all-reduce.5 = f32[4096]{0:T(1024)S(1)} all-reduce(f32[4096]{0:T(1024)S(1)} %dynamic-update-slice.6), channel_id=5, replica_groups=mesh['ta'=4,'gz'=8,'xy'=8] {'ta','gz','xy'}, use_global_device_ids=true, to_apply=%add.5 | all-reduce | flops 4096 | bytes 32768
  816.4 8.8 %custom-call.9 = f32[16,6,6]{2,1,0:T(8,128)S(1)} custom-call(f32[16,6,6]{2,1,0:T(8,128)S(1)} %fusion.88), custom_call_target="Cholesky" | custom-call | tf_op jit(solution)/shard_map/jit(cholesky)/cholesky | solution.py:84
  825.5 7.6 custom-call.10
  (158 shorter events, 26.2 us)
Async XLA Ops:
  0.0 100.6 %copy-start = (bf16[2,2,2,2,9,64,128]{6,5,4,3,2,1,0:T(8,128)(2,1)S(1)}, bf16[2,2,2,2,9,64,128]{6,5,4,3,2,1,0:T(8,128)(2,1)}, u32[]{:S(2)}) copy-start(bf16[2,2,2,2,9,64,128]{6,5,4,3,2,1,0:T(8,128)(2,1)} %param.3) | copy-start | bytes 7077892
  83.9 2.8 collective-permute-start
  84.5 4.0 collective-permute-start.1
  88.5 5.2 collective-permute-start.2
  90.7 3.0 collective-permute-start.3
  93.8 3.9 collective-permute-start.4
  94.4 5.0 collective-permute-start.5
  100.6 1.2 copy-start.1
  251.8 3.4 collective-permute-start.6
  254.1 4.0 collective-permute-start.7
  258.2 3.7 collective-permute-start.8
  260.3 1.6 collective-permute-start.9
  261.9 3.9 collective-permute-start.10
  262.9 5.0 collective-permute-start.11
  495.5 3.5 collective-permute-start.12
  498.0 4.0 collective-permute-start.13
  502.0 3.7 collective-permute-start.14
  504.1 1.6 collective-permute-start.15
  505.8 4.2 collective-permute-start.16
  507.6 5.0 collective-permute-start.17
